TPU v7x, 128 devices: a whole 4x4x4 slice. The times are simulated.
128 devices in a mesh: scan: 8 (over x, y_lo), det: 16 (over y_hi, z, core).
Axes of the slice: x: 4, y: 4 (y_hi: 2, y_lo: 2; y = y_hi * 2 + y_lo), z: 4, core: 2. Of those that a mesh axis runs over, the one named last changes fastest.
Arguments:
- data: float32 [2, 512, 2, 256, 256], P(None, 'scan', None, 'det'), may hold values from -6 to 6
- wigner: float32 [2, 512, 2, 256, 256], P(None, ('scan', 'det')), may hold values from -6 to 6
Outputs:
- deconvolved: float32 [2, 512, 2, 256, 256], P(None, 'scan', None, 'det')
All inputs are finite; a program needn't handle non-finite values.
Results may differ from a plain program's by a relative error of at most 0.0001.
Values sent between devices are 32-bit elements; how exact they have to be, the bound alone decides.
No kernel may reach another device: no remote copies, remote signals or barrier semaphores. Data moves between devices by JAX's collectives and lax.ppermute only.
A program may use at most 128 MiB of HBM per device.

v0:
```python
import math

import jax
import numpy as np
import jax.numpy as jnp
from jax import lax
from jax.sharding import PartitionSpec as P

eps_wiener = 0.1
MATMUL_PRECISION = lax.Precision.HIGH


def angles(rows, cols, count):
    product = (rows[:, None] * cols[None, :]) % count
    return product * (2.0 * np.pi / count)


def tables(count, sign):
    indices = np.arange(count)
    phases = angles(indices, indices, count)
    norm_scale = 1.0 / np.sqrt(count)
    return (np.cos(phases) * norm_scale, sign * np.sin(phases) * norm_scale)


def row_table(rows_total, blocks):
    local = rows_total // blocks
    q = np.arange(rows_total)[:, None]
    r = np.arange(rows_total)[None, :]
    phases = ((q * r) % rows_total) * (2.0 * np.pi / rows_total)
    cosine = np.cos(phases) / np.sqrt(rows_total)
    sines = np.sin(phases) / np.sqrt(rows_total)
    full = np.stack([np.stack([cosine, sines], axis=1), np.stack([-sines, cosine], axis=1)], axis=1)
    full = full.reshape(rows_total, 2, 2, blocks, local).transpose(0, 1, 3, 2, 4)
    return jnp.asarray(full.reshape(2 * rows_total, 2 * rows_total).astype(np.float32))


def product_form(form, left, right):
    return jnp.einsum(form, left, right, precision=MATMUL_PRECISION)


def pair_right(real_in, imag_in, form, cosine, sines):
    real_out = product_form(form, real_in, cosine) - product_form(form, imag_in, sines)
    imag_out = product_form(form, real_in, sines) + product_form(form, imag_in, cosine)
    return (real_out, imag_out)


def complex_table(cosine, sines):
    return jnp.asarray(np.block([[cosine, sines], [-sines, cosine]]).astype(np.float32))


def shards(data, wigner):
    n_scan = lax.axis_size("scan")
    n_det = lax.axis_size("det")
    n_all = n_scan * n_det
    _, local_rows, freq_count, local_det, detector = data.shape
    rows_total = local_rows * n_scan
    det_total = local_det * n_det
    q_block = rows_total // n_all
    frame_count = q_block * freq_count
    row_parts = max(1, min(local_det // 8, n_scan // freq_count))
    col_parts = n_scan // (freq_count * row_parts)
    row_sub = local_det // row_parts
    col_sub = detector // col_parts

    send = data.reshape(2, local_rows, freq_count, row_parts, row_sub, col_parts, col_sub)
    send = send.transpose(2, 3, 5, 0, 1, 4, 6).reshape(n_scan, 2 * local_rows, row_sub, col_sub)
    got = lax.all_to_all(send, "scan", 0, 0, tiled=True)
    got = got.reshape(2 * rows_total, row_sub, col_sub)

    spectra = jnp.einsum("pk,kmn->pmn", row_table(rows_total, n_scan), got, precision=MATMUL_PRECISION)
    spectra = spectra.reshape(n_all, q_block * 2, row_sub, col_sub)

    frames = lax.all_to_all(spectra, ("scan", "det"), 0, 0, tiled=True)
    frames = frames.reshape(freq_count, row_parts, col_parts, n_det, q_block, 2, row_sub, col_sub)
    frames = frames.transpose(4, 0, 1, 3, 6, 5, 2, 7).reshape(frame_count * det_total, 2 * detector)

    pos = np.arange(det_total)
    h_of = pos // (n_det * row_sub)
    d_of = (pos // row_sub) % n_det
    a_of = local_det * d_of + row_sub * h_of + pos % row_sub
    cols = np.arange(detector)
    scale = 1.0 / np.sqrt(detector)
    row_phase = angles(a_of, cols, detector)
    inv_cos, inv_sin = tables(detector, 1.0)
    fwd_cos, fwd_sin = tables(detector, -1.0)

    half = jnp.dot(frames, complex_table(inv_cos, inv_sin), precision=MATMUL_PRECISION)
    half = half.reshape(frame_count, det_total, 2, detector).transpose(0, 3, 2, 1)
    half = half.reshape(frame_count * detector, 2 * det_total)
    perm_table = complex_table(np.cos(row_phase) * scale, np.sin(row_phase) * scale)
    field = jnp.dot(half, perm_table, precision=MATMUL_PRECISION)
    field_real = field[:, :detector]
    field_imag = field[:, detector:]
    kernel_real = wigner[0].reshape(frame_count * detector, detector)
    kernel_imag = wigner[1].reshape(frame_count * detector, detector)
    power = kernel_real * kernel_real + kernel_imag * kernel_imag + eps_wiener
    filtered_real = (field_real * kernel_real + field_imag * kernel_imag) / power
    filtered_imag = (field_imag * kernel_real - field_real * kernel_imag) / power
    filtered = jnp.concatenate([filtered_real, filtered_imag], axis=1)

    fwd_table = complex_table(fwd_cos, fwd_sin)
    half = jnp.dot(filtered, fwd_table, precision=MATMUL_PRECISION)
    half = half.reshape(q_block, freq_count, detector, 2 * det_total)
    plane_real, plane_imag = pair_right(
        half[..., :det_total], half[..., det_total:], "qfya,by->qfab",
        jnp.asarray(fwd_cos.astype(np.float32)), jnp.asarray(fwd_sin.astype(np.float32)),
    )
    planes = jnp.stack([plane_real, plane_imag])

    planes = planes.reshape(2, q_block, freq_count, n_det, local_det, detector)
    planes = planes.transpose(3, 0, 1, 2, 4, 5).reshape(n_det, 2 * q_block * freq_count * local_det, detector)
    back = lax.all_to_all(planes, "det", 0, 0, tiled=True)
    back = back.reshape(n_det, 2, q_block, freq_count, local_det, detector).transpose(1, 0, 2, 3, 4, 5)
    return back.reshape(2, n_det * q_block, freq_count, local_det, detector)


def solution(mesh):
    in_specs = (P(None, "scan", None, "det", None), P(None, ("scan", "det"), None, None, None))
    out_specs = P(None, "scan", None, "det", None)
    return jax.shard_map(shards, mesh=mesh, in_specs=in_specs, out_specs=out_specs, check_vma=False)
```

profile of v0, /device:TPU:1, one launch (start us, length us, event | category | flops | bytes accessed | tf_op | source)
XLA Modules:
  0.0 229.7 jit_solution(1079203934394867128)
XLA Ops:
  0.0 4.6 %copy.28 = f32[2,64,2,2,8,2,128]{6,1,0,4,5,3,2:T(8,128)S(1)} copy(f32[2,64,2,2,8,2,128]{6,4,5,3,2,1,0:T(8,128)} %bitcast.102) | data formatting | bytes 8388608 | tf_op jit(solution)/shard_map/reshape | solution.py:65
  4.6 54.2 %all_to_all.15 = f32[8,128,8,128]{3,1,2,0:T(8,128)S(1)} all-to-all(f32[8,128,8,128]{3,1,2,0:T(8,128)S(1)} %bitcast.99), channel_id=1, replica_groups=mesh['scan'=8,'det'=16] {'scan'}, dimensions={0} | all-to-all | bytes 8388608 | tf_op jit(solution)/shard_map/all_to_all | solution.py:67
  58.8 0.5 copy.29
  59.3 1.7 copy-done.7
  61.0 6.7 %fusion.21 = f32[128,8,8,128]{3,0,2,1:T(8,128)S(1)} fusion(f32[128,8,1024,1]{2,0,3,1:T(8,128)S(1)} %copy-done.7, f32[1024,8,128,1]{2,0,1,3:T(8,128)S(1)} %bitcast.103), kind=kOutput, calls=%fused_computation.26 | convolution fusion | flops 6442450944 | bytes 12582912 | tf_op jit(solution)/shard_map/pk,kmn->pmn/dot_general | solution.py:70
  67.7 4.4 %copy.30 = f32[128,8,8,128]{3,2,1,0:T(8,128)} copy(f32[128,8,8,128]{3,0,2,1:T(8,128)S(1)} %fusion.21) | data formatting | bytes 8388608 | tf_op jit(solution)/shard_map/pk,kmn->pmn/dot_general | solution.py:70
  72.2 11.0 %all-to-all-start.1 = ((f32[128,8,8,128]{3,2,1,0:T(8,128)}), f32[128,8,8,128]{3,2,1,0:T(8,128)}, u32[]{:S(2)}, u32[]{:S(2)}) async-start(f32[128,8,8,128]{3,2,1,0:T(8,128)} %copy.30), calls=%async_computation.1 | async-start | bytes 8388608 | tf_op jit(solution)/shard_map/all_to_all | solution.py:73
  83.2 3.9 %fusion.20 = (f32[1,4,2,256,256]{4,3,2,1,0:T(8,128)S(1)}, f32[1,4,2,256,256]{4,3,2,1,0:T(8,128)}) fusion(f32[2,4,2,256,256]{4,3,2,1,0:T(8,128)} %param.9), kind=kLoop, calls=%fused_computation.25 | loop fusion | bytes 8388608 | tf_op jit(solution)/shard_map/slice | solution.py:94
  87.1 48.1 %all-to-all-done.1 = f32[128,8,8,128]{3,2,1,0:T(8,128)} async-done(((f32[128,8,8,128]{3,2,1,0:T(8,128)}), f32[128,8,8,128]{3,2,1,0:T(8,128)}, u32[]{:S(2)}, u32[]{:S(2)}) %all-to-all-start.1) | async-done | bytes 4194336 | tf_op jit(solution)/shard_map/all_to_all | solution.py:73
  135.2 2.9 %copy.31 = f32[2,2,2,16,4,2,8,128]{7,6,2,5,3,1,0,4:T(8,128)S(1)} copy(f32[2,2,2,16,4,2,8,128]{7,6,5,4,3,2,1,0:T(8,128)} %bitcast.7) | data formatting | bytes 8388608 | tf_op jit(solution)/shard_map/reshape | solution.py:74
  138.1 3.5 %convolution_bitcast_fusion = f32[8,256,2,256]{1,3,2,0:T(8,128)S(1)} fusion(f32[8,256,512,1]{2,1,3,0:T(8,128)S(1)} %bitcast.94, f32[2,256,512,1]{2,1,0,3:T(8,128)S(1)} %copy-done.2), kind=kOutput, calls=%fused_computation.2 | convolution fusion | flops 3221225472 | bytes 9437184 | tf_op jit(solution)/shard_map/dot_general | solution.py:87
  141.5 2.4 %copy.32 = f32[8,256,2,256]{1,0,3,2:T(8,128)S(1)} copy(f32[8,256,2,256]{1,3,2,0:T(8,128)S(1)} %convolution_bitcast_fusion) | data formatting | bytes 8388608 | tf_op jit(solution)/shard_map/transpose | solution.py:88
  144.0 2.0 copy.45
  146.0 13.2 %fusion.22 = f32[2048,512]{1,0:T(8,128)S(1)} fusion(f32[2048,512]{0,1:T(8,128)S(1)} %bitcast.95, f32[512,512]{1,0:T(8,128)S(1)} %copy-done.1), kind=kOutput, calls=%fused_computation.27 | convolution fusion | flops 3221225472 | bytes 9437184 | tf_op jit(solution)/shard_map/dot_general | solution.py:91
  159.2 0.9 fusion.5
  160.3 1.9 fusion.23
  162.2 1.9 convolution_add_fusion
  164.2 1.9 fusion.6
  166.0 1.9 fusion.8
  167.9 1.9 fusion.17
  169.8 1.9 fusion.14
  171.7 0.6 pad_maximum_fusion
  172.8 54.2 %all_to_all.16 = f32[16,256,256]{2,1,0:T(8,128)S(1)} all-to-all(f32[16,256,256]{2,1,0:T(8,128)S(1)} %bitcast.97), channel_id=1, replica_groups=mesh['scan'=8,'det'=16] {'det'}, dimensions={0} | all-to-all | bytes 8388608 | tf_op jit(solution)/shard_map/all_to_all | solution.py:112
  227.0 2.5 %copy.37 = f32[2,16,4,2,16,256]{5,4,3,2,1,0:T(8,128)} copy(f32[2,16,4,2,16,256]{5,4,3,2,0,1:T(8,128)S(1)} %bitcast.98) | data formatting | bytes 8388608 | tf_op jit(solution)/shard_map/transpose | solution.py:113
  (16 shorter events, 0.6 us)
Async XLA Ops:
  58.8 2.2 copy-start.7
  72.2 63.0 %all-to-all-start.1 = ((f32[128,8,8,128]{3,2,1,0:T(8,128)}), f32[128,8,8,128]{3,2,1,0:T(8,128)}, u32[]{:S(2)}, u32[]{:S(2)}) async-start(f32[128,8,8,128]{3,2,1,0:T(8,128)} %copy.30), calls=%async_computation.1 | async-start | bytes 8388608 | tf_op jit(solution)/shard_map/all_to_all | solution.py:73
  135.2 2.9 %copy-start.2 = (f32[2,256,512,1]{2,1,0,3:T(8,128)S(1)}, f32[2,256,512,1]{2,1,0,3:T(8,128)}, u32[]{:S(2)}) copy-start(f32[2,256,512,1]{2,1,0,3:T(8,128)} %constant.27) | copy-start | bytes 3145732
  144.0 2.0 copy-start.1
  146.0 13.2 %copy-start = (f32[1,4,2,256,256]{4,3,2,1,0:T(8,128)S(1)}, f32[1,4,2,256,256]{4,3,2,1,0:T(8,128)}, u32[]{:S(2)}) copy-start(f32[1,4,2,256,256]{4,3,2,1,0:T(8,128)} %get-tuple-element.8) | copy-start | bytes 6291460
  159.2 1.0 copy-start.5
  160.2 2.0 copy-start.6
  162.2 2.0 copy-start.3
  164.1 1.9 copy-start.4
where the time goes:
time: 234 us; the launch traced here: 230 us
  blocking collectives  108 us (46%)
  waiting for transfers between devices  48.1 us (21%)
  matrix products  34.8 us (15%)
  local copies, waits for them, and re-layouts  25.5 us (11%)
  starting transfers between devices  11 us (5%)
    all_to_all x1, blocking collectives, shards(): back = lax.all_to_all(planes, 'det', 0, 0, tiled=True)  54.2 us
    all_to_all x1, blocking collectives, shards(): got = lax.all_to_all(send, 'scan', 0, 0, tiled=True)  54.2 us
    all_to_all x1, waiting for transfers between devices, shards(): frames = lax.all_to_all(spectra, ('scan', 'det'), 0, 0, tiled=True)  48.1 us
    dot_general x1, matrix products, shards(): field = jnp.dot(half, perm_table, precision=MATMUL_PRECISION)  13.2 us
    all_to_all x1, starting transfers between devices, shards(): frames = lax.all_to_all(spectra, ('scan', 'det'), 0, 0, tiled=True)  11 us
    dot_general x4, matrix products, product_form(): return jnp.einsum(form, left, right, precision=MATMUL_PRECISION)  7.51 us
    dot_general x1, matrix products, shards(): jnp.einsum('pk,kmn->pmn', row_table(rows_total, n_scan), got, precision=M...  6.74 us
  transfers between devices with their start and end apart: 1, of which 1 were waited for; matrix products, arithmetic and copies ran while one was open for 2% of the time, Pallas kernels for 0%

commit v1 on v0

--- a/solution.py
+++ b/solution.py
@@ -71,6 +71,7 @@
     spectra = spectra.reshape(n_all, q_block * 2, row_sub, col_sub)
 
     frames = lax.all_to_all(spectra, ("scan", "det"), 0, 0, tiled=True)
+    frames, wigner = lax.optimization_barrier((frames, wigner))
     frames = frames.reshape(freq_count, row_parts, col_parts, n_det, q_block, 2, row_sub, col_sub)
     frames = frames.transpose(4, 0, 1, 3, 6, 5, 2, 7).reshape(frame_count * det_total, 2 * detector)
 

time: 234 us -> 232 us (level)
  blocking collectives: 108 us -> 171 us
  waiting for transfers between devices: 48.1 us -> 0 us
  starting transfers between devices: 11 us -> 0 us
  local copies, waits for them, and re-layouts: 25.5 us -> 19.5 us
    all_to_all x0 -> x1, blocking collectives: none -> 62.7 us  [shards(): frames = lax.all_to_all(spectra, ('scan', 'det'), 0, 0, tiled=True)]
    all_to_all x1 -> x0, waiting for transfers between devices: 48.1 us -> none  [shards(): frames = lax.all_to_all(spectra, ('scan', 'det'), 0, 0, tiled=True)]
    all_to_all x1 -> x0, starting transfers between devices: 11 us -> none  [shards(): frames = lax.all_to_all(spectra, ('scan', 'det'), 0, 0, tiled=True)]
    slice x1, local copies, waits for them, and re-layouts: 3.95 us -> 0.45 us  [shards(): kernel_real = wigner[0].reshape(frame_count * detector, detector)]
    reshape x1 -> x0, local copies, waits for them, and re-layouts: 2.86 us -> none  [shards(): frames.reshape(freq_count, row_parts, col_parts, n_det, q_block, 2, row_s...]
  transfers between devices with their start and end apart: 1 -> 0, of which waited for: 1 -> 0; matrix products, arithmetic and copies ran while one was open for 2% -> 0% of each run, Pallas kernels for 0% -> 0%
where the time goes in v1:
time: 232 us; the launch traced here: 227 us
  blocking collectives  171 us (74%)
  matrix products  34.8 us (15%)
  local copies, waits for them, and re-layouts  19.5 us (8%)
    all_to_all x1, blocking collectives, shards(): frames = lax.all_to_all(spectra, ('scan', 'det'), 0, 0, tiled=True)  62.7 us
    all_to_all x1, blocking collectives, shards(): back = lax.all_to_all(planes, 'det', 0, 0, tiled=True)  54.2 us
    all_to_all x1, blocking collectives, shards(): got = lax.all_to_all(send, 'scan', 0, 0, tiled=True)  54.2 us
    dot_general x1, matrix products, shards(): field = jnp.dot(half, perm_table, precision=MATMUL_PRECISION)  13.2 us
    dot_general x4, matrix products, product_form(): return jnp.einsum(form, left, right, precision=MATMUL_PRECISION)  7.52 us
    dot_general x1, matrix products, shards(): jnp.einsum('pk,kmn->pmn', row_table(rows_total, n_scan), got, precision=M...  6.74 us
    unnamed x17, local copies, waits for them, and re-layouts  5.42 us

profile of v1, /device:TPU:1, one launch (start us, length us, event | category | flops | bytes accessed | tf_op | source)
XLA Modules:
  0.0 227.3 jit_solution(10007317140366074068)
XLA Ops:
  0.0 4.6 %copy.28 = f32[2,64,2,2,8,2,128]{6,1,0,4,5,3,2:T(8,128)S(1)} copy(f32[2,64,2,2,8,2,128]{6,4,5,3,2,1,0:T(8,128)} %bitcast.103) | data formatting | bytes 8388608 | tf_op jit(solution)/shard_map/reshape | solution.py:65
  4.6 54.2 %all_to_all.15 = f32[8,128,8,128]{3,1,2,0:T(8,128)S(1)} all-to-all(f32[8,128,8,128]{3,1,2,0:T(8,128)S(1)} %bitcast.100), channel_id=1, replica_groups=mesh['scan'=8,'det'=16] {'scan'}, dimensions={0} | all-to-all | bytes 8388608 | tf_op jit(solution)/shard_map/all_to_all | solution.py:67
  59.3 1.7 copy-done.7
  61.0 6.7 %fusion.21 = f32[128,8,8,128]{3,0,2,1:T(8,128)S(1)} fusion(f32[128,8,1024,1]{2,0,3,1:T(8,128)S(1)} %copy-done.7, f32[1024,8,128,1]{2,0,1,3:T(8,128)S(1)} %bitcast.104), kind=kOutput, calls=%fused_computation.26 | convolution fusion | flops 6442450944 | bytes 12582912 | tf_op jit(solution)/shard_map/pk,kmn->pmn/dot_general | solution.py:70
  67.7 2.4 %copy.30 = f32[128,8,8,128]{3,2,1,0:T(8,128)S(1)} copy(f32[128,8,8,128]{3,0,2,1:T(8,128)S(1)} %fusion.21) | data formatting | bytes 8388608 | tf_op jit(solution)/shard_map/pk,kmn->pmn/dot_general | solution.py:70
  70.2 62.7 %all_to_all.16 = f32[128,8,8,128]{3,2,1,0:T(8,128)S(1)} all-to-all(f32[128,8,8,128]{3,2,1,0:T(8,128)S(1)} %copy.30), channel_id=1, replica_groups=mesh['scan'=8,'det'=16] {'scan','det'}, dimensions={0} | all-to-all | bytes 8388608 | tf_op jit(solution)/shard_map/all_to_all | solution.py:73
  132.9 0.6 copy.31
  133.5 0.6 copy-done.2
  134.1 3.5 %convolution_bitcast_fusion = f32[8,256,2,256]{1,3,2,0:T(8,128)S(1)} fusion(f32[8,256,512,1]{2,1,3,0:T(8,128)S(1)} %bitcast.95, f32[2,256,512,1]{2,1,0,3:T(8,128)S(1)} %copy-done.2), kind=kOutput, calls=%fused_computation.2 | convolution fusion | flops 3221225472 | bytes 9437184 | tf_op jit(solution)/shard_map/dot_general | solution.py:88
  137.6 2.4 %copy.32 = f32[8,256,2,256]{1,0,3,2:T(8,128)S(1)} copy(f32[8,256,2,256]{1,3,2,0:T(8,128)S(1)} %convolution_bitcast_fusion) | data formatting | bytes 8388608 | tf_op jit(solution)/shard_map/transpose | solution.py:89
  140.0 2.0 copy.45
  142.7 0.8 copy-done.1
  143.4 13.2 %fusion.22 = f32[2048,512]{1,0:T(8,128)S(1)} fusion(f32[2048,512]{0,1:T(8,128)S(1)} %bitcast.94, f32[512,512]{1,0:T(8,128)S(1)} %copy-done.1), kind=kOutput, calls=%fused_computation.27 | convolution fusion | flops 3221225472 | bytes 9437184 | tf_op jit(solution)/shard_map/dot_general | solution.py:92
  156.7 0.9 fusion.5
  157.7 1.9 fusion.23
  159.7 1.9 convolution_add_fusion
  161.6 1.9 fusion.6
  163.5 1.9 fusion.8
  165.4 1.9 fusion.17
  167.3 1.9 fusion.14
  169.2 0.6 pad_maximum_fusion
  169.8 0.6 copy.42
  170.4 54.2 %all_to_all.17 = f32[16,256,256]{2,1,0:T(8,128)S(1)} all-to-all(f32[16,256,256]{2,1,0:T(8,128)S(1)} %bitcast.98), channel_id=1, replica_groups=mesh['scan'=8,'det'=16] {'det'}, dimensions={0} | all-to-all | bytes 8388608 | tf_op jit(solution)/shard_map/all_to_all | solution.py:113
  224.7 2.5 %copy.37 = f32[2,16,4,2,16,256]{5,4,3,2,1,0:T(8,128)} copy(f32[2,16,4,2,16,256]{5,4,3,2,0,1:T(8,128)S(1)} %bitcast.99) | data formatting | bytes 8388608 | tf_op jit(solution)/shard_map/transpose | solution.py:114
  (15 shorter events, 1.3 us)
Async XLA Ops:
  58.8 2.2 copy-start.7
  132.9 1.2 copy-start.2
  140.0 2.2 copy-start
  142.2 1.2 copy-start.1
  156.7 1.0 copy-start.5
  157.6 2.0 copy-start.6
  159.6 2.0 copy-start.3
  161.6 1.9 copy-start.4

commit v2 on v1

--- a/solution.py
+++ b/solution.py
@@ -86,10 +86,13 @@
     fwd_cos, fwd_sin = tables(detector, -1.0)
 
     half = jnp.dot(frames, complex_table(inv_cos, inv_sin), precision=MATMUL_PRECISION)
-    half = half.reshape(frame_count, det_total, 2, detector).transpose(0, 3, 2, 1)
-    half = half.reshape(frame_count * detector, 2 * det_total)
-    perm_table = complex_table(np.cos(row_phase) * scale, np.sin(row_phase) * scale)
-    field = jnp.dot(half, perm_table, precision=MATMUL_PRECISION)
+    half = half.reshape(frame_count, det_total * 2, detector)
+    perm_cos = np.cos(row_phase) * scale
+    perm_sin = np.sin(row_phase) * scale
+    perm_table = np.stack([np.concatenate([perm_cos, perm_sin], 1), np.concatenate([-perm_sin, perm_cos], 1)], 1)
+    perm_table = jnp.asarray(perm_table.reshape(det_total * 2, 2 * detector).astype(np.float32))
+    field = jnp.einsum("zky,kx->zyx", half, perm_table, precision=MATMUL_PRECISION)
+    field = field.reshape(frame_count * detector, 2 * detector)
     field_real = field[:, :detector]
     field_imag = field[:, detector:]
     kernel_real = wigner[0].reshape(frame_count * detector, detector)

time: 232 us -> 228 us (0.983); the launches traced: 227 us -> 227 us
  local copies, waits for them, and re-layouts: 19.5 us -> 27.5 us
  matrix products: 34.8 us -> 27 us
    reshape x0 -> x2, local copies, waits for them, and re-layouts: none -> 10.3 us  [shards(): half = half.reshape(frame_count, det_total * 2, detector)]
    dot_general x1, matrix products: 13.2 us -> 3.74 us  [shards(): jnp.einsum('zky,kx->zyx', half, perm_table, precision=MATMUL_PRECISION)]
    transpose x1 -> x0, local copies, waits for them, and re-layouts: 2.43 us -> none  [shards(): half.reshape(frame_count, det_total, 2, detector).transpose(0, 3, 2, 1)]
    slice x1, local copies, waits for them, and re-layouts: 0.45 us -> 2.78 us  [shards(): kernel_real = wigner[0].reshape(frame_count * detector, detector)]
    unnamed x17 -> x16, local copies, waits for them, and re-layouts: 5.42 us -> 3.43 us
where the time goes in v2:
time: 228 us; the launch traced here: 227 us
  blocking collectives  171 us (75%)
  local copies, waits for them, and re-layouts  27.5 us (12%)
  matrix products  27 us (12%)
    all_to_all x1, blocking collectives, shards(): frames = lax.all_to_all(spectra, ('scan', 'det'), 0, 0, tiled=True)  62.7 us
    all_to_all x1, blocking collectives, shards(): back = lax.all_to_all(planes, 'det', 0, 0, tiled=True)  54.2 us
    all_to_all x1, blocking collectives, shards(): got = lax.all_to_all(send, 'scan', 0, 0, tiled=True)  54.2 us
    reshape x2, local copies, waits for them, and re-layouts, shards(): half = half.reshape(frame_count, det_total * 2, detector)  10.3 us
    dot_general x4, matrix products, product_form(): return jnp.einsum(form, left, right, precision=MATMUL_PRECISION)  7.73 us
    dot_general x1, matrix products, shards(): jnp.einsum('pk,kmn->pmn', row_table(rows_total, n_scan), got, precision=M...  6.74 us
    dot_general x1, matrix products, shards(): jnp.dot(frames, complex_table(inv_cos, inv_sin), precision=MATMUL_PRECISION)  4.95 us
    reshape x1, local copies, waits for them, and re-layouts, shards(): data.reshape(2, local_rows, freq_count, row_parts, row_sub, col_parts, co...  4.62 us

profile of v2, /device:TPU:1, one launch (start us, length us, event | category | flops | bytes accessed | tf_op | source)
XLA Modules:
  0.0 227.3 jit_solution(4771616663642982555)
XLA Ops:
  0.0 4.6 %copy.36 = f32[2,64,2,2,8,2,128]{6,1,0,4,5,3,2:T(8,128)S(1)} copy(f32[2,64,2,2,8,2,128]{6,4,5,3,2,1,0:T(8,128)} %bitcast.93) | data formatting | bytes 8388608 | tf_op jit(solution)/shard_map/reshape | solution.py:65
  4.6 54.2 %all_to_all.15 = f32[8,128,8,128]{3,1,2,0:T(8,128)S(1)} all-to-all(f32[8,128,8,128]{3,1,2,0:T(8,128)S(1)} %bitcast.90), channel_id=1, replica_groups=mesh['scan'=8,'det'=16] {'scan'}, dimensions={0} | all-to-all | bytes 8388608 | tf_op jit(solution)/shard_map/all_to_all | solution.py:67
  59.3 1.7 copy-done.7
  61.0 6.7 %fusion.21 = f32[128,8,8,128]{3,0,2,1:T(8,128)S(1)} fusion(f32[128,8,1024,1]{2,0,3,1:T(8,128)S(1)} %copy-done.7, f32[1024,8,128,1]{2,0,1,3:T(8,128)S(1)} %bitcast.94), kind=kOutput, calls=%fused_computation.25 | convolution fusion | flops 6442450944 | bytes 12582912 | tf_op jit(solution)/shard_map/pk,kmn->pmn/dot_general | solution.py:70
  67.7 2.4 %copy.38 = f32[128,8,8,128]{3,2,1,0:T(8,128)S(1)} copy(f32[128,8,8,128]{3,0,2,1:T(8,128)S(1)} %fusion.21) | data formatting | bytes 8388608 | tf_op jit(solution)/shard_map/pk,kmn->pmn/dot_general | solution.py:70
  70.2 62.7 %all_to_all.16 = f32[128,8,8,128]{3,2,1,0:T(8,128)S(1)} all-to-all(f32[128,8,8,128]{3,2,1,0:T(8,128)S(1)} %copy.38), channel_id=1, replica_groups=mesh['scan'=8,'det'=16] {'scan','det'}, dimensions={0} | all-to-all | bytes 8388608 | tf_op jit(solution)/shard_map/all_to_all | solution.py:73
  132.9 0.6 copy.39
  133.5 0.6 copy-done.2
  134.1 4.9 %fusion.22 = f32[2048,512]{1,0:T(8,128)} fusion(f32[2048,512]{1,0:T(8,128)S(1)} %bitcast.86, f32[512,512]{1,0:T(8,128)S(1)} %copy-done.2), kind=kOutput, calls=%fused_computation.26 | convolution fusion | flops 3221225472 | bytes 9437184 | tf_op jit(solution)/shard_map/dot_general | solution.py:88
  139.1 4.9 %reshape.44 = f32[8,512,256]{2,1,0:T(8,128)} reshape(f32[2048,512]{1,0:T(8,128)} %fusion.22) | data formatting | bytes 8388608 | tf_op jit(solution)/shard_map/reshape | solution.py:89
  144.0 5.3 %copy.40 = f32[8,512,256]{1,2,0:T(8,128)} copy(f32[8,512,256]{2,1,0:T(8,128)} %reshape.44) | data formatting | bytes 8388608 | tf_op jit(solution)/shard_map/reshape | solution.py:89
  149.3 2.8 %fusion.20 = (f32[1,4,2,256,256]{4,3,2,1,0:T(8,128)S(1)}, f32[1,4,2,256,256]{4,3,2,1,0:T(8,128)S(1)}) fusion(f32[2,4,2,256,256]{4,3,2,1,0:T(8,128)} %param.9), kind=kLoop, calls=%fused_computation.24 | loop fusion | bytes 8388608 | tf_op jit(solution)/shard_map/slice | solution.py:98
  152.1 0.7 copy-done
  153.1 3.7 %fusion.23 = f32[2048,512]{1,0:T(8,128)S(1)} fusion(f32[2048,512]{1,0:T(8,128)S(1)} %bitcast.85, f32[512,512]{1,0:T(8,128)S(1)} %copy-done.1), kind=kOutput, calls=%fused_computation.27 | convolution fusion | flops 3221225472 | bytes 9437184 | tf_op jit(solution)/shard_map/zky,kx->zyx/dot_general | solution.py:94
  156.8 0.9 fusion.5
  157.8 1.9 fusion.24
  159.8 1.9 convolution_add_fusion
  161.7 1.9 fusion.6
  163.6 1.9 fusion.8
  165.5 2.1 fusion.17
  167.6 1.9 fusion.14
  169.5 0.6 pad_maximum_fusion
  170.6 54.2 %all_to_all.17 = f32[16,256,256]{2,1,0:T(8,128)S(1)} all-to-all(f32[16,256,256]{2,1,0:T(8,128)S(1)} %bitcast.88), channel_id=1, replica_groups=mesh['scan'=8,'det'=16] {'det'}, dimensions={0} | all-to-all | bytes 8388608 | tf_op jit(solution)/shard_map/all_to_all | solution.py:116
  224.8 2.5 %copy.45 = f32[2,16,4,2,16,256]{5,4,3,2,1,0:T(8,128)} copy(f32[2,16,4,2,16,256]{5,4,3,2,0,1:T(8,128)S(1)} %bitcast.89) | data formatting | bytes 8388608 | tf_op jit(solution)/shard_map/transpose | solution.py:117
  (15 shorter events, 1.4 us)
Async XLA Ops:
  58.8 2.2 copy-start.7
  132.9 1.2 copy-start.2
  149.3 3.4 %copy-start = (f32[8,512,256]{1,2,0:T(8,128)S(1)}, f32[8,512,256]{1,2,0:T(8,128)}, u32[]{:S(2)}) copy-start(f32[8,512,256]{1,2,0:T(8,128)} %copy.40) | copy-start | bytes 12582916
  149.3 3.7 %copy-start.1 = (f32[512,512]{1,0:T(8,128)S(1)}, f32[512,512]{1,0:T(8,128)}, u32[]{:S(2)}) copy-start(f32[512,512]{1,0:T(8,128)} %constant.16.clone) | copy-start | bytes 3145732
  156.8 1.0 copy-start.5
  157.7 2.0 copy-start.6
  159.8 2.0 copy-start.3
  161.7 1.9 copy-start.4

commit v3 on v1

--- a/solution.py
+++ b/solution.py
@@ -102,10 +102,10 @@
     fwd_table = complex_table(fwd_cos, fwd_sin)
     half = jnp.dot(filtered, fwd_table, precision=MATMUL_PRECISION)
     half = half.reshape(q_block, freq_count, detector, 2 * det_total)
-    plane_real, plane_imag = pair_right(
-        half[..., :det_total], half[..., det_total:], "qfya,by->qfab",
-        jnp.asarray(fwd_cos.astype(np.float32)), jnp.asarray(fwd_sin.astype(np.float32)),
-    )
+    both = jnp.asarray(np.concatenate([fwd_cos, fwd_sin], axis=1).astype(np.float32))
+    parts = jnp.einsum("qfyp,yn->qfpn", half, both, precision=MATMUL_PRECISION)
+    plane_real = parts[:, :, :det_total, :detector] - parts[:, :, det_total:, detector:]
+    plane_imag = parts[:, :, det_total:, :detector] + parts[:, :, :det_total, detector:]
     planes = jnp.stack([plane_real, plane_imag])
 
     planes = planes.reshape(2, q_block, freq_count, n_det, local_det, detector)

time: 232 us -> 215 us (0.927); the launches traced: 227 us -> 214 us
  matrix products: 34.8 us -> 21.6 us
    dot_general x1, matrix products: 13.2 us -> 3.94 us  [shards(): field = jnp.dot(half, perm_table, precision=MATMUL_PRECISION)]
    dot_general x4 -> x1, matrix products: 7.52 us -> 3.57 us  [shards(): parts = jnp.einsum('qfyp,yn->qfpn', half, both, precision=MATMUL_PRECISION)]
    unnamed x17 -> x15, local copies, waits for them, and re-layouts: 5.42 us -> 5.41 us
where the time goes in v3:
time: 215 us; the launch traced here: 214 us
  blocking collectives  171 us (80%)
  matrix products  21.6 us (10%)
  local copies, waits for them, and re-layouts  19.5 us (9%)
    all_to_all x1, blocking collectives, shards(): frames = lax.all_to_all(spectra, ('scan', 'det'), 0, 0, tiled=True)  62.7 us
    all_to_all x1, blocking collectives, shards(): back = lax.all_to_all(planes, 'det', 0, 0, tiled=True)  54.2 us
    all_to_all x1, blocking collectives, shards(): got = lax.all_to_all(send, 'scan', 0, 0, tiled=True)  54.2 us
    dot_general x1, matrix products, shards(): jnp.einsum('pk,kmn->pmn', row_table(rows_total, n_scan), got, precision=M...  6.74 us
    unnamed x15, local copies, waits for them, and re-layouts  5.41 us
    reshape x1, local copies, waits for them, and re-layouts, shards(): data.reshape(2, local_rows, freq_count, row_parts, row_sub, col_parts, co...  4.62 us

profile of v3, /device:TPU:1, one launch (start us, length us, event | category | flops | bytes accessed | tf_op | source)
XLA Modules:
  0.0 214.4 jit_solution(13993081660812529384)
XLA Ops:
  0.0 4.6 %copy.24 = f32[2,64,2,2,8,2,128]{6,1,0,4,5,3,2:T(8,128)S(1)} copy(f32[2,64,2,2,8,2,128]{6,4,5,3,2,1,0:T(8,128)} %bitcast.95) | data formatting | bytes 8388608 | tf_op jit(solution)/shard_map/reshape | solution.py:65
  4.6 54.2 %all_to_all.15 = f32[8,128,8,128]{3,1,2,0:T(8,128)S(1)} all-to-all(f32[8,128,8,128]{3,1,2,0:T(8,128)S(1)} %bitcast.92), channel_id=1, replica_groups=mesh['scan'=8,'det'=16] {'scan'}, dimensions={0} | all-to-all | bytes 8388608 | tf_op jit(solution)/shard_map/all_to_all | solution.py:67
  58.8 0.5 copy.25
  59.3 1.7 copy-done.6
  61.0 6.7 %fusion.7 = f32[128,8,8,128]{3,0,2,1:T(8,128)S(1)} fusion(f32[128,8,1024,1]{2,0,3,1:T(8,128)S(1)} %copy-done.6, f32[1024,8,128,1]{2,0,1,3:T(8,128)S(1)} %bitcast.96), kind=kOutput, calls=%fused_computation.18 | convolution fusion | flops 6442450944 | bytes 12582912 | tf_op jit(solution)/shard_map/pk,kmn->pmn/dot_general | solution.py:70
  67.7 2.4 %copy.26 = f32[128,8,8,128]{3,2,1,0:T(8,128)S(1)} copy(f32[128,8,8,128]{3,0,2,1:T(8,128)S(1)} %fusion.7) | data formatting | bytes 8388608 | tf_op jit(solution)/shard_map/pk,kmn->pmn/dot_general | solution.py:70
  70.2 62.7 %all_to_all.16 = f32[128,8,8,128]{3,2,1,0:T(8,128)S(1)} all-to-all(f32[128,8,8,128]{3,2,1,0:T(8,128)S(1)} %copy.26), channel_id=1, replica_groups=mesh['scan'=8,'det'=16] {'scan','det'}, dimensions={0} | all-to-all | bytes 8388608 | tf_op jit(solution)/shard_map/all_to_all | solution.py:73
  132.9 0.6 copy.27
  133.5 0.6 copy-done.2
  134.1 3.5 %convolution_bitcast_fusion = f32[8,256,2,256]{1,3,2,0:T(8,128)S(1)} fusion(f32[8,256,512,1]{2,1,3,0:T(8,128)S(1)} %bitcast.87, f32[2,256,512,1]{2,1,0,3:T(8,128)S(1)} %copy-done.2), kind=kOutput, calls=%fused_computation.2 | convolution fusion | flops 3221225472 | bytes 9437184 | tf_op jit(solution)/shard_map/dot_general | solution.py:88
  137.6 2.4 %copy.28 = f32[8,256,2,256]{1,0,3,2:T(8,128)S(1)} copy(f32[8,256,2,256]{1,3,2,0:T(8,128)S(1)} %convolution_bitcast_fusion) | data formatting | bytes 8388608 | tf_op jit(solution)/shard_map/transpose | solution.py:89
  140.0 2.0 copy.38
  142.2 0.5 fusion.6
  142.7 0.8 copy-done.1
  143.4 3.9 %fusion.8 = f32[2048,512]{1,0:T(8,128)S(1)} fusion(f32[2048,512]{0,1:T(8,128)S(1)} %bitcast.86, f32[512,512]{1,0:T(8,128)S(1)} %copy-done.1), kind=kOutput, calls=%fused_computation.19 | convolution fusion | flops 3221225472 | bytes 9437184 | tf_op jit(solution)/shard_map/dot_general | solution.py:92
  147.4 0.9 fusion.5
  148.4 1.9 fusion.9
  150.3 2.0 convolution_add_fusion
  152.3 3.6 %fusion.10 = f32[4,2,512,512]{3,2,1,0:T(8,128)S(1)} fusion(f32[4,2,256,512]{3,2,1,0:T(8,128)S(1)} %bitcast.85, f32[256,512,1,1]{1,0,3,2:T(8,128)S(1)} %copy-done.5), kind=kOutput, calls=%fused_computation.21 | convolution fusion | flops 3221225472 | bytes 13107200 | tf_op jit(solution)/shard_map/qfyp,yn->qfpn/dot_general | solution.py:106
  155.9 0.6 slice_subtract_fusion
  156.5 0.5 pad_maximum_fusion
  157.0 0.6 copy.37
  157.7 54.2 %all_to_all.17 = f32[16,256,256]{2,1,0:T(8,128)S(1)} all-to-all(f32[16,256,256]{2,1,0:T(8,128)S(1)} %bitcast.90), channel_id=1, replica_groups=mesh['scan'=8,'det'=16] {'det'}, dimensions={0} | all-to-all | bytes 8388608 | tf_op jit(solution)/shard_map/all_to_all | solution.py:113
  211.9 2.5 %copy.32 = f32[2,16,4,2,16,256]{5,4,3,2,1,0:T(8,128)} copy(f32[2,16,4,2,16,256]{5,4,3,2,0,1:T(8,128)S(1)} %bitcast.91) | data formatting | bytes 8388608 | tf_op jit(solution)/shard_map/transpose | solution.py:114
  (11 shorter events, 0.3 us)
Async XLA Ops:
  58.8 2.2 %copy-start.6 = (f32[128,8,1024,1]{2,0,3,1:T(8,128)S(1)}, f32[128,8,1024,1]{2,0,3,1:T(8,128)}, u32[]{:S(2)}) copy-start(f32[128,8,1024,1]{2,0,3,1:T(8,128)} %constant.23) | copy-start | bytes 12582916
  132.9 1.2 copy-start.2
  140.0 2.2 %copy-start = (f32[2,4,2,256,256]{4,3,2,1,0:T(8,128)S(1)}, f32[2,4,2,256,256]{4,3,2,1,0:T(8,128)}, u32[]{:S(2)}) copy-start(f32[2,4,2,256,256]{4,3,2,1,0:T(8,128)} %param.8) | copy-start | bytes 12582916
  142.2 1.2 copy-start.1
  147.4 1.0 copy-start.3
  148.3 2.0 copy-start.4
  150.3 2.0 copy-start.5

commit v4 on v3

--- a/solution.py
+++ b/solution.py
@@ -86,12 +86,11 @@
     fwd_cos, fwd_sin = tables(detector, -1.0)
 
     half = jnp.dot(frames, complex_table(inv_cos, inv_sin), precision=MATMUL_PRECISION)
-    half = half.reshape(frame_count, det_total, 2, detector).transpose(0, 3, 2, 1)
-    half = half.reshape(frame_count * detector, 2 * det_total)
-    perm_table = complex_table(np.cos(row_phase) * scale, np.sin(row_phase) * scale)
-    field = jnp.dot(half, perm_table, precision=MATMUL_PRECISION)
-    field_real = field[:, :detector]
-    field_imag = field[:, detector:]
+    half = half.reshape(frame_count, det_total, 2 * detector)
+    perm_both = np.concatenate([np.cos(row_phase) * scale, np.sin(row_phase) * scale], axis=1)
+    parts = jnp.einsum("zap,an->zpn", half, jnp.asarray(perm_both.astype(np.float32)), precision=MATMUL_PRECISION)
+    field_real = (parts[:, :detector, :detector] - parts[:, detector:, detector:]).reshape(-1, detector)
+    field_imag = (parts[:, :detector, detector:] + parts[:, detector:, :detector]).reshape(-1, detector)
     kernel_real = wigner[0].reshape(frame_count * detector, detector)
     kernel_imag = wigner[1].reshape(frame_count * detector, detector)
     power = kernel_real * kernel_real + kernel_imag * kernel_imag + eps_wiener

time: 215 us -> 211 us (0.981)
  local copies, waits for them, and re-layouts: 19.5 us -> 15.6 us
    transpose x1 -> x0, local copies, waits for them, and re-layouts: 2.43 us -> none  [shards(): half.reshape(frame_count, det_total, 2, detector).transpose(0, 3, 2, 1)]
    unnamed x15 -> x14, local copies, waits for them, and re-layouts: 5.41 us -> 4.04 us
where the time goes in v4:
time: 211 us
  blocking collectives  171 us (81%)
  matrix products  21.5 us (10%)
  local copies, waits for them, and re-layouts  15.6 us (7%)
  other arithmetic  2.6 us (1%)
    all_to_all x1, blocking collectives, shards(): frames = lax.all_to_all(spectra, ('scan', 'det'), 0, 0, tiled=True)  62.7 us
    all_to_all x1, blocking collectives, shards(): back = lax.all_to_all(planes, 'det', 0, 0, tiled=True)  54.2 us
    all_to_all x1, blocking collectives, shards(): got = lax.all_to_all(send, 'scan', 0, 0, tiled=True)  54.2 us
    dot_general x1, matrix products, shards(): jnp.einsum('pk,kmn->pmn', row_table(rows_total, n_scan), got, precision=M...  6.74 us
    reshape x1, local copies, waits for them, and re-layouts, shards(): data.reshape(2, local_rows, freq_count, row_parts, row_sub, col_parts, co...  4.62 us

profile of v4, /device:TPU:1, one launch (start us, length us, event | category | flops | bytes accessed | tf_op | source)
XLA Modules:
  0.0 211.0 jit_solution(11143377242948870598)
XLA Ops:
  0.0 4.6 %copy.30 = f32[2,64,2,2,8,2,128]{6,1,0,4,5,3,2:T(8,128)S(1)} copy(f32[2,64,2,2,8,2,128]{6,4,5,3,2,1,0:T(8,128)} %bitcast.89) | data formatting | bytes 8388608 | tf_op jit(solution)/shard_map/reshape | solution.py:65
  4.6 54.2 %all_to_all.15 = f32[8,128,8,128]{3,1,2,0:T(8,128)S(1)} all-to-all(f32[8,128,8,128]{3,1,2,0:T(8,128)S(1)} %bitcast.86), channel_id=1, replica_groups=mesh['scan'=8,'det'=16] {'scan'}, dimensions={0} | all-to-all | bytes 8388608 | tf_op jit(solution)/shard_map/all_to_all | solution.py:67
  58.8 0.5 copy.31
  59.3 1.7 copy-done.6
  61.0 6.7 %fusion.7 = f32[128,8,8,128]{3,0,2,1:T(8,128)S(1)} fusion(f32[128,8,1024,1]{2,0,3,1:T(8,128)S(1)} %copy-done.6, f32[1024,8,128,1]{2,0,1,3:T(8,128)S(1)} %bitcast.90), kind=kOutput, calls=%fused_computation.19 | convolution fusion | flops 6442450944 | bytes 12582912 | tf_op jit(solution)/shard_map/pk,kmn->pmn/dot_general | solution.py:70
  67.7 2.4 %copy.32 = f32[128,8,8,128]{3,2,1,0:T(8,128)S(1)} copy(f32[128,8,8,128]{3,0,2,1:T(8,128)S(1)} %fusion.7) | data formatting | bytes 8388608 | tf_op jit(solution)/shard_map/pk,kmn->pmn/dot_general | solution.py:70
  70.2 62.7 %all_to_all.16 = f32[128,8,8,128]{3,2,1,0:T(8,128)S(1)} all-to-all(f32[128,8,8,128]{3,2,1,0:T(8,128)S(1)} %copy.32), channel_id=1, replica_groups=mesh['scan'=8,'det'=16] {'scan','det'}, dimensions={0} | all-to-all | bytes 8388608 | tf_op jit(solution)/shard_map/all_to_all | solution.py:73
  132.9 0.6 copy.33
  133.5 0.6 copy-done.1
  134.1 3.5 %fusion.8 = f32[8,256,512]{1,2,0:T(8,128)S(1)} fusion(f32[8,256,512]{2,1,0:T(8,128)S(1)} %bitcast.82, f32[512,512,1]{1,0,2:T(8,128)S(1)} %copy-done.1), kind=kOutput, calls=%fused_computation.20 | convolution fusion | flops 3221225472 | bytes 9437184 | tf_op jit(solution)/shard_map/dot_general | solution.py:88
  137.6 3.6 %fusion.9 = f32[8,512,512]{2,1,0:T(8,128)S(1)} fusion(f32[8,256,512]{1,2,0:T(8,128)S(1)} %fusion.8, f32[256,512,1]{1,0,2:T(8,128)S(1)} %copy-done.2), kind=kOutput, calls=%fused_computation.21 | convolution fusion | flops 3221225472 | bytes 13107200 | tf_op jit(solution)/shard_map/zap,an->zpn/dot_general | solution.py:91
  141.2 0.6 slice_subtract_fusion.1
  141.8 1.6 copy-done
  143.4 0.4 fusion.6
  143.8 0.9 fusion.5
  144.7 0.1 copy-done.3
  144.8 1.9 fusion.10
  146.7 2.2 %convolution_add_fusion = f32[2048,512]{1,0:T(8,128)S(1)} fusion(f32[2048,512]{1,0:T(8,128)S(1)} %fusion.10, f32[2048,256]{1,0:T(8,128)S(1)} %get-tuple-element.11, f32[256,512]{1,0:T(8,128)S(1)} %copy-done.4), kind=kOutput, calls=%fused_computation.1 | convolution fusion | flops 1611661312 | bytes 11010048 | tf_op jit(solution)/shard_map/dot_general | solution.py:102
  149.0 3.6 %fusion.11 = f32[4,2,512,512]{3,2,1,0:T(8,128)S(1)} fusion(f32[4,2,256,512]{3,2,1,0:T(8,128)S(1)} %bitcast.81, f32[256,512,1,1]{1,0,3,2:T(8,128)S(1)} %copy-done.5), kind=kOutput, calls=%fused_computation.23 | convolution fusion | flops 3221225472 | bytes 13107200 | tf_op jit(solution)/shard_map/qfyp,yn->qfpn/dot_general | solution.py:105
  152.5 0.6 slice_subtract_fusion
  153.2 0.5 pad_maximum_fusion
  153.6 0.6 copy.43
  154.3 54.2 %all_to_all.17 = f32[16,256,256]{2,1,0:T(8,128)S(1)} all-to-all(f32[16,256,256]{2,1,0:T(8,128)S(1)} %bitcast.84), channel_id=1, replica_groups=mesh['scan'=8,'det'=16] {'det'}, dimensions={0} | all-to-all | bytes 8388608 | tf_op jit(solution)/shard_map/all_to_all | solution.py:112
  208.5 2.5 %copy.38 = f32[2,16,4,2,16,256]{5,4,3,2,1,0:T(8,128)} copy(f32[2,16,4,2,16,256]{5,4,3,2,0,1:T(8,128)S(1)} %bitcast.85) | data formatting | bytes 8388608 | tf_op jit(solution)/shard_map/transpose | solution.py:113
  (10 shorter events, 0.0 us)
Async XLA Ops:
  58.8 2.2 %copy-start.6 = (f32[128,8,1024,1]{2,0,3,1:T(8,128)S(1)}, f32[128,8,1024,1]{2,0,3,1:T(8,128)}, u32[]{:S(2)}) copy-start(f32[128,8,1024,1]{2,0,3,1:T(8,128)} %constant.21) | copy-start | bytes 12582916
  132.9 1.2 copy-start.1
  134.1 3.5 %copy-start.2 = (f32[256,512,1]{1,0,2:T(8,128)S(1)}, f32[256,512,1]{1,0,2:T(8,128)}, u32[]{:S(2)}) copy-start(f32[256,512,1]{1,0,2:T(8,128)} %constant.23) | copy-start | bytes 1572868
  141.2 2.2 %copy-start = (f32[2,4,2,256,256]{4,3,2,1,0:T(8,128)S(1)}, f32[2,4,2,256,256]{4,3,2,1,0:T(8,128)}, u32[]{:S(2)}) copy-start(f32[2,4,2,256,256]{4,3,2,1,0:T(8,128)} %param.8) | copy-start | bytes 12582916
  143.8 1.0 copy-start.3
  144.7 2.0 copy-start.4
  146.7 2.2 %copy-start.5 = (f32[256,512,1,1]{1,0,3,2:T(8,128)S(1)}, f32[256,512,1,1]{1,0,3,2:T(8,128)}, u32[]{:S(2)}) copy-start(f32[256,512,1,1]{1,0,3,2:T(8,128)} %constant.24) | copy-start | bytes 1572868
